TPU v7x, 32 devices: a whole 2x2x4 slice. The times are simulated.
32 devices in a mesh: grp: 2 (over x), chan: 16 (over z, y, core).
Axes of the slice: x: 2, y: 2, z: 4, core: 2. Of those that a mesh axis runs over, the one named last changes fastest.
Arguments:
- samples: bfloat16 [128, 62, 8192], P('chan', 'grp'), parts along dimension 1, may hold values from -6 to 6
- eq_gain: float32 [128, 4096], P('chan'), may hold values from 0.5 to 2
- delays: float32 [1024, 64], replicated, may hold values from -64 to 64
Outputs:
- beams: bfloat16 [2, 1024, 4096], P('grp', 'chan'), parts along dimension 0
There are 2 independent parts, one for each index of `grp`. A program takes and returns all parts, laid end to end along the dimension named above; an argument that names none is the same for every part. Nothing has to cross between parts.
All inputs are finite; a program needn't handle non-finite values.
Results may differ from a plain program's by a relative error of at most 0.0034.
Values may be sent and summed in bfloat16 or wider, within the bound.
No kernel may reach another device: no remote copies, remote signals or barrier semaphores. Data moves between devices by JAX's collectives and lax.ppermute only.
A program may use at most 448 MiB of HBM per device.

v0:
```python
import math
import jax
import jax.numpy as jnp
from jax import lax
from jax.sharding import PartitionSpec as P

DISHES = 64
POLS = 2
NB = 1024
TAPS = 16
AVG = 16
SPEC = 16


def pfb_taps(frame_len, tap_count):
    tap_total = tap_count * frame_len
    position = jnp.arange(tap_total, dtype=jnp.float32) + 0.5
    window = 0.5 - 0.5 * jnp.cos(2.0 * math.pi / tap_total * position)
    offset = (position - 0.5 * tap_total) / frame_len
    prototype = window * jnp.sin(math.pi * offset) / (math.pi * offset)
    prototype = prototype / jnp.sqrt(jnp.sum(prototype * prototype))
    return prototype.reshape(tap_count, frame_len)


def cos_sin(numer, denom):
    phase_angle = 2.0 * math.pi / denom * numer.astype(jnp.float32)
    return (jnp.cos(phase_angle), -jnp.sin(phase_angle))


def turn_tables(frame_len):
    outer_len = 2 ** ((frame_len.bit_length() - 1) // 2)
    inner_len = frame_len // outer_len
    half_len = inner_len // 2
    outer_index = jnp.arange(outer_len, dtype=jnp.int32)
    inner_index = jnp.arange(inner_len, dtype=jnp.int32)
    half_index = jnp.arange(half_len, dtype=jnp.int32)
    one_cos, one_sin = cos_sin(outer_index[:, None] * outer_index[None, :] % outer_len, outer_len)
    twist_cos, twist_sin = cos_sin(
        outer_index[:, None] * inner_index[None, :] % frame_len, frame_len
    )
    three_cos, three_sin = cos_sin(
        inner_index[:, None] * half_index[None, :] % inner_len, inner_len
    )
    table_one = jnp.stack([one_cos, one_sin])
    table_three = jnp.stack([three_cos, three_sin])
    return (outer_len, inner_len, table_one, twist_cos, twist_sin, table_three)


def body(samples, eq_gain, delays):
    inputs_here, frame_count, frame_len = samples.shape
    chan_count = frame_len // 2
    groups = lax.axis_size("chan")
    my_index = lax.axis_index("chan")
    chan_here = chan_count // groups
    beams_here = NB // groups
    time_bins = SPEC // AVG
    highest = lax.Precision.HIGHEST
    tap_table = pfb_taps(frame_len, TAPS)
    filtered = jnp.zeros((inputs_here, SPEC, frame_len), jnp.float32)
    for tap_index in range(TAPS):
        filtered = filtered + tap_table[tap_index] * samples[
            :, tap_index : tap_index + SPEC, :
        ].astype(jnp.float32)
    outer_len, inner_len, table_one, twist_cos, twist_sin, table_three = turn_tables(frame_len)
    framed = filtered.reshape(inputs_here, SPEC, outer_len, inner_len)
    section_one = jnp.einsum("rkn,isnm->irskm", table_one, framed, precision=highest)
    real_one = section_one[:, 0]
    imag_one = section_one[:, 1]
    twisted = jnp.stack(
        [real_one * twist_cos - imag_one * twist_sin, real_one * twist_sin + imag_one * twist_cos],
        axis=1,
    )
    section_three = jnp.einsum("irskm,qmj->irqsjk", twisted, table_three, precision=highest)
    spec_real = (section_three[:, 0, 0] - section_three[:, 1, 1]).reshape(
        inputs_here, SPEC, chan_count
    )
    spec_imag = (section_three[:, 0, 1] + section_three[:, 1, 0]).reshape(
        inputs_here, SPEC, chan_count
    )
    gain_row = eq_gain[:, None, :]
    voltages = jnp.stack(
        [(spec_real * gain_row).astype(jnp.bfloat16), (spec_imag * gain_row).astype(jnp.bfloat16)],
        axis=1,
    )
    row_width = chan_here * inputs_here * 2 * AVG
    outgoing = (
        voltages.reshape(inputs_here, 2, time_bins, AVG, chan_count)
        .transpose(2, 4, 0, 1, 3)
        .reshape(time_bins, groups, row_width)
    )
    channel = (my_index * chan_here + jnp.arange(chan_here, dtype=jnp.int32)).astype(jnp.float32)
    phase_turns = channel[:, None, None] * delays[None, :, :] / frame_len
    phase_angle = 2.0 * math.pi * phase_turns
    weight_scale = 1.0 / math.sqrt(DISHES)
    w_real = (jnp.cos(phase_angle) * weight_scale).astype(jnp.bfloat16)
    w_imag = (-jnp.sin(phase_angle) * weight_scale).astype(jnp.bfloat16)
    weight_stack = jnp.stack(
        [jnp.stack([w_real, -w_imag], axis=-1), jnp.stack([w_imag, w_real], axis=-1)], axis=1
    )
    block_count = math.gcd(chan_here, 8)
    block_len = chan_here // block_count
    weight_blocks = weight_stack.reshape(block_count, block_len, 2, NB, DISHES, 2)
    arrived = lax.all_to_all(outgoing, "chan", split_axis=1, concat_axis=1, tiled=True)
    item_count = arrived.shape[0]
    volt_grid = arrived.reshape(item_count, groups, chan_here, inputs_here, 2, AVG)
    volt_grid = volt_grid.transpose(2, 1, 3, 4, 0, 5).reshape(
        block_count, block_len, DISHES, POLS, 2, item_count, AVG
    )

    def one_block(block_pair):
        weight_part, volt_part = block_pair
        product = jnp.einsum(
            "cobdr,cdprqa->cobpqa", weight_part, volt_part, preferred_element_type=jnp.float32
        )
        return jnp.sum(product * product, axis=(1, 3, 5)) / AVG

    energy = lax.map(one_block, (weight_blocks, volt_grid))
    power_bins = energy.reshape(chan_here, NB, item_count).transpose(2, 1, 0).astype(jnp.bfloat16)
    sending = power_bins.reshape(item_count, groups, beams_here * chan_here)
    landed = lax.all_to_all(sending, "chan", split_axis=1, concat_axis=1, tiled=True)
    return (
        landed.reshape(time_bins, groups, beams_here, chan_here)
        .transpose(0, 2, 1, 3)
        .reshape(time_bins, beams_here, chan_count)
    )


def solution(mesh):
    in_specs = (P("chan", "grp", None), P("chan", None), P())
    out_specs = P("grp", "chan", None)
    return jax.shard_map(body, mesh=mesh, in_specs=in_specs, out_specs=out_specs, check_vma=False)
```

profile of v0, /device:TPU:0, one launch (start us, length us, event | category | flops | bytes accessed | tf_op | source)
XLA Modules:
  0.0 906.9 jit_solution(4844415604220031745)
XLA Ops:
  9.0 16.7 %add_bitcast_fusion = f32[8,16,64,128,1]{3,0,2,1,4:T(8,128)S(1)} fusion(bf16[8,31,8192]{2,0,1:T(8,128)(2,1)} %param.5, f32[8192]{0:T(1024)S(1)} %get-tuple-element.53, f32[8192]{0:T(1024)S(1)} %get-tuple-element.54, f32[8192]{0:T(1024)S(1)} %get-tuple-element.55, f32[8192]{0:T(1024)S(1)} %get-tuple-element.56, f32[8192]{0:T(1024)S(1)} %get-tuple-element.57, ...), kind=kLoop, calls=%fused_computation.26 | loop fusion | flops 49283072 | bytes 38273024 | tf_op jit(solution)/shard_map/reshape | solution.py:65
  25.8 7.2 fusion.18
  35.1 27.6 %fusion.12 = f32[8,2,2,16,64,64]{5,4,3,1,0,2:T(8,128)} fusion(f32[1,128,64]{1,2,0:T(8,128)S(1)} %get-tuple-element.76, f32[1,128,64]{1,2,0:T(8,128)S(1)} %get-tuple-element.77, f32[8,1,16,64,128]{4,3,1,2,0:T(8,128)S(1)} %get-tuple-element.51, f32[8,1,16,64,128]{4,3,1,2,0:T(8,128)S(1)} %get-tuple-element.50), kind=kOutput, calls=%fused_computation.18 | convolution fusion | flops 3223339008 | bytes 16842752 | tf_op jit(solution)/shard_map/irskm,qmj->irqsjk/dot_general | solution.py:73
  62.6 12.0 %slice_subtract_fusion = (f32[8,1,1,16,64,64]{5,4,3,1,0,2:T(8,128)}, f32[8,1,1,16,64,64]{5,4,3,1,0,2:T(8,128)}) fusion(f32[8,2,2,16,64,64]{5,4,3,1,0,2:T(8,128)} %fusion.12), kind=kLoop, calls=%fused_computation.21 | loop fusion | flops 1048576 | bytes 12582912 | tf_op jit(solution)/shard_map/sub | solution.py:74
  85.2 27.8 %copy.27 = bf16[1,4096,8,2,16]{4,3,2,1,0:T(2,128)(2,1)} copy(bf16[1,4096,8,2,16]{1,4,3,2,0:T(8,128)(2,1)S(1)} %maximum_bitcast_fusion) | data formatting | bytes 4194304 | tf_op jit(solution)/shard_map/transpose | solution.py:88
  113.0 18.3 %reshape.393 = bf16[1,16,65536]{2,0,1:T(2,128)(2,1)} reshape(bf16[1,4096,8,2,16]{4,3,2,1,0:T(2,128)(2,1)} %copy.27) | data formatting | bytes 4194304 | tf_op jit(solution)/shard_map/reshape | solution.py:89
  131.9 13.0 %reduce.6 = bf16[16,65536]{1,0:T(8,128)(2,1)S(1)} reduce(bf16[16,1,65536]{2,1,0:T(2,128)(2,1)} %bitcast.92, bf16[]{:T(256)} %broadcast.400), dimensions={1}, to_apply=%bitcast.78.reduce_sub_computation | reduce | bytes 4194306
  147.8 7.3 all-to-all-start
  155.2 251.5 %multiply_convert_fusion = (bf16[8,32,1,1024,64,1]{3,4,5,2,1,0:T(8,128)(2,1)}, bf16[8,32,1,1024,64,1]{3,4,5,2,1,0:T(8,128)(2,1)}) fusion(f32[1024,64]{0,1:T(8,128)S(1)} %copy-done, f32[8,32]{1,0:T(8,128)S(1)} %add_convert_fusion), kind=kLoop, calls=%fused_computation.11 | loop fusion | flops 117440512 | bytes 67372032 | tf_op jit(solution)/shard_map/convert_element_type | solution.py:96
  406.7 229.4 %fusion.15 = bf16[8,32,1,1024,64,1]{3,4,5,2,1,0:T(8,128)(2,1)} fusion(f32[1024,64]{0,1:T(8,128)S(1)} %copy-done, f32[8,32]{1,0:T(8,128)S(1)} %add_convert_fusion), kind=kLoop, calls=%fused_computation.19 | loop fusion | flops 134217728 | bytes 33817600 | tf_op jit(solution)/shard_map/neg | solution.py:98
  636.1 86.9 %maximum_maximum_fusion = bf16[8,32,2,1024,64,2]{3,4,5,2,1,0:T(8,128)(2,1)} fusion(bf16[8,32,1,1024,64,1]{3,4,5,2,1,0:T(8,128)(2,1)} %get-tuple-element.69, bf16[8,32,1,1024,64,1]{3,4,5,2,1,0:T(8,128)(2,1)} %get-tuple-element.68, bf16[8,32,1,1024,64,1]{3,4,5,2,1,0:T(8,128)(2,1)} %fusion.15), kind=kLoop, calls=%fused_computation.10 | loop fusion | flops 201326592 | bytes 234881024 | tf_op jit(solution)/shard_map/stack | solution.py:97
  729.8 13.2 %bitcast_reduce_fusion = bf16[16,65536]{1,0:T(8,128)(2,1)S(1)} fusion(bf16[16,1,65536]{2,1,0:T(2,128)(2,1)} %reshape.398), kind=kLoop, calls=%fused_computation.91 | loop fusion | bytes 4194304 | tf_op jit(solution)/shard_map/all_to_all | solution.py:103
  743.0 20.1 %reshape.381 = bf16[1,16,256,8,2,16]{5,4,3,2,1,0:T(2,128)(2,1)} reshape(bf16[16,65536]{1,0:T(8,128)(2,1)S(1)} %bitcast_reduce_fusion) | data formatting | bytes 4194304 | tf_op jit(solution)/shard_map/reshape | solution.py:105
  763.1 35.2 %copy.29 = bf16[256,16,8,2,1,16]{0,5,3,2,1,4:T(8,128)(2,1)S(1)} copy(bf16[256,16,8,2,1,16]{5,3,2,0,1,4:T(2,128)(2,1)} %bitcast.91) | data formatting | bytes 4194304 | tf_op jit(solution)/shard_map/transpose | solution.py:106
  804.5 13.3 %copy.30 = bf16[8,32,64,2,2,1,16]{2,6,4,3,1,5,0:T(8,128)(2,1)} copy(bf16[8,32,64,2,2,1,16]{1,0,6,4,3,2,5:T(8,128)(2,1)} %reshape.382) | data formatting | bytes 4194304 | tf_op jit(solution)/shard_map/while | solution.py:117
  817.8 59.0 %while.10 = (s32[]{:T(128)}, bf16[8,32,1024,1]{2,3,1,0:T(2,128)(2,1)S(1)}, bf16[8,32,2,1024,64,2]{3,4,5,2,1,0:T(8,128)(2,1)}, bf16[8,32,64,2,2,1,16]{2,6,4,3,1,5,0:T(8,128)(2,1)}, s32[]{:T(128)}) while((s32[]{:T(128)}, bf16[8,32,1024,1]{2,3,1,0:T(2,128)(2,1)S(1)}, bf16[8,32,2,1024,64,2]{3,4,5,2,1,0:T(8,128)(2,1)}, ...), condition=%wide.region_3.4_spmd, body=%wide.region_1.3_spmd.sunk | while | flops 541097984 | bytes 17826888 | solution.py:117
  825.2 7.2 fusion.68
  832.6 7.3 fusion.68
  839.9 7.3 fusion.68
  847.3 7.2 fusion.68
  854.7 7.2 fusion.68
  862.1 7.3 fusion.68
  869.5 7.3 fusion.68
  881.9 20.3 %all_to_all.10 = bf16[16,2,8192]{2,1,0:T(2,128)(2,1)S(1)} all-to-all(bf16[16,2,8192]{2,1,0:T(2,128)(2,1)S(1)} %reshape.399), channel_id=1, replica_groups=mesh['grp'=2,'chan'=16] {'chan'}, dimensions={0} | all-to-all | bytes 1048576 | tf_op jit(solution)/shard_map/all_to_all | solution.py:120
  (49 shorter events, 54.8 us)
Async XLA Ops:
  78.2 4.8 copy-start.1
  144.9 10.3 %copy-start = (f32[1024,64]{0,1:T(8,128)S(1)}, f32[1024,64]{0,1:T(8,128)}, u32[]{:S(2)}) copy-start(f32[1024,64]{0,1:T(8,128)} %param.7) | copy-start | bytes 786436
  147.8 575.2 %all-to-all-start = ((bf16[16,2,32768]{2,1,0:T(2,128)(2,1)}), bf16[16,2,32768]{2,1,0:T(2,128)(2,1)S(1)}, u32[]{:S(2)}, u32[]{:S(2)}) async-start(bf16[16,2,32768]{2,1,0:T(2,128)(2,1)} %reshape.397), calls=%async_computation | async-start | bytes 4194304 | tf_op jit(solution)/shard_map/all_to_all | solution.py:103
where the time goes:
time: 916 us; the launch traced here: 907 us
  other arithmetic  626 us (68%)
  local copies, waits for them, and re-layouts  159 us (17%)
  matrix products  92.8 us (10%)
  blocking collectives  20.3 us (2%)
    convert_element_type x1, other arithmetic, body(): w_imag = (-jnp.sin(phase_angle) * weight_scale).astype(jnp.bfloat16)  251 us
    neg x1, other arithmetic, body(): -w_imag  229 us
    another operation x1, other arithmetic, body(): jnp.stack([jnp.stack([w_real, -w_imag], axis=-1), jnp.stack([w_imag, w_re...  86.9 us
    dot_general x8, matrix products, one_block(): jnp.einsum('cobdr,cdprqa->cobpqa', weight_part, volt_part, preferred_elem...  58 us
    transpose x1, local copies, waits for them, and re-layouts, body(): volt_grid.transpose(2, 1, 3, 4, 0, 5)  35.2 us
    transpose x1, local copies, waits for them, and re-layouts, body(): outgoing = voltages.reshape(inputs_here, 2, time_bins, AVG, chan_count).t...  27.8 us
    dot_general x1, matrix products, body(): jnp.einsum('irskm,qmj->irqsjk', twisted, table_three, precision=highest)  27.6 us
    all_to_all x1, blocking collectives, body(): lax.all_to_all(sending, 'chan', split_axis=1, concat_axis=1, tiled=True)  20.3 us
  transfers between devices with their start and end apart: 1, of which 0 were waited for; matrix products, arithmetic and copies ran while one was open for 63% of the time, Pallas kernels for 0%

commit v1 on v0

--- a/solution.py
+++ b/solution.py
@@ -10,6 +10,26 @@
 TAPS = 16
 AVG = 16
 SPEC = 16
+
+
+def pack_tables(mesh_dim, mine):
+    local_now, lower = (lax.axis_size(mesh_dim), lax.axis_index(mesh_dim))
+    x_new = mine.shape[1] // local_now
+    y1 = list(mine.shape)
+    y1[1] = x_new
+    tall = y1[1]
+    y1[1] = tall * local_now
+    aux = jnp.zeros(y1, mine.dtype)
+    kk = 0
+    while kk < local_now:
+        z_new = lax.dynamic_slice_in_dim(mine, (lower ^ kk) * x_new, x_new, axis=1)
+        if kk:
+            z_new = lax.ppermute(
+                z_new, axis_name=mesh_dim, perm=tuple(((j0, j0 ^ kk) for j0 in range(local_now)))
+            )
+        aux = lax.dynamic_update_slice_in_dim(aux, z_new, (lower ^ kk) * tall, axis=1)
+        kk = kk + 1
+    return aux
 
 
 def pfb_taps(frame_len, tap_count):
@@ -100,7 +120,7 @@
     block_count = math.gcd(chan_here, 8)
     block_len = chan_here // block_count
     weight_blocks = weight_stack.reshape(block_count, block_len, 2, NB, DISHES, 2)
-    arrived = lax.all_to_all(outgoing, "chan", split_axis=1, concat_axis=1, tiled=True)
+    arrived = pack_tables("chan", outgoing)
     item_count = arrived.shape[0]
     volt_grid = arrived.reshape(item_count, groups, chan_here, inputs_here, 2, AVG)
     volt_grid = volt_grid.transpose(2, 1, 3, 4, 0, 5).reshape(

time: 916 us -> 1020 us (1.11)
  local copies, waits for them, and re-layouts: 159 us -> 253 us
  starting transfers between devices: 7.35 us -> 22.4 us
  other arithmetic: 626 us -> 612 us
    dynamic_update_slice x0 -> x16, local copies, waits for them, and re-layouts: none -> 87.4 us  [pack_tables(): lax.dynamic_update_slice_in_dim(aux, z_new, (lower ^ kk) * tall, axis=1)]
    ppermute x0 -> x15, starting transfers between devices: none -> 22.4 us  [pack_tables(): lax.ppermute(z_new, axis_name=mesh_dim, perm=tuple(((j0, j0 ^ kk) for j0...]
    reshape x1, local copies, waits for them, and re-layouts: 18.3 us -> 40.3 us  [body(): outgoing = voltages.reshape(inputs_here, 2, time_bins, AVG, chan_count).t...]
    all_to_all x1 -> x0, local copies, waits for them, and re-layouts: 13.2 us -> none  [body(): lax.all_to_all(outgoing, 'chan', split_axis=1, concat_axis=1, tiled=True)]
    unnamed x2 -> x1, other arithmetic: 16.7 us -> 3.79 us
  transfers between devices with their start and end apart: 1 -> 15, of which waited for: 0 -> 0; matrix products, arithmetic and copies ran while one was open for 63% -> 65% of each run, Pallas kernels for 0% -> 0%
where the time goes in v1:
time: 1020 us; the launch traced here: 1000 us
  other arithmetic  612 us (60%)
  local copies, waits for them, and re-layouts  253 us (25%)
  matrix products  93.1 us (9%)
  starting transfers between devices  22.4 us (2%)
  blocking collectives  19.4 us (2%)
    convert_element_type x1, other arithmetic, body(): w_imag = (-jnp.sin(phase_angle) * weight_scale).astype(jnp.bfloat16)  251 us
    neg x1, other arithmetic, body(): -w_imag  229 us
    dynamic_update_slice x16, local copies, waits for them, and re-layouts, pack_tables(): lax.dynamic_update_slice_in_dim(aux, z_new, (lower ^ kk) * tall, axis=1)  87.4 us
    another operation x1, other arithmetic, body(): jnp.stack([jnp.stack([w_real, -w_imag], axis=-1), jnp.stack([w_imag, w_re...  86.9 us
    dot_general x8, matrix products, one_block(): jnp.einsum('cobdr,cdprqa->cobpqa', weight_part, volt_part, preferred_elem...  58 us
    reshape x1, local copies, waits for them, and re-layouts, body(): outgoing = voltages.reshape(inputs_here, 2, time_bins, AVG, chan_count).t...  40.3 us
    transpose x1, local copies, waits for them, and re-layouts, body(): volt_grid.transpose(2, 1, 3, 4, 0, 5)  35.2 us
    transpose x1, local copies, waits for them, and re-layouts, body(): outgoing = voltages.reshape(inputs_here, 2, time_bins, AVG, chan_count).t...  27.9 us
  transfers between devices with their start and end apart: 15, of which 0 were waited for; matrix products, arithmetic and copies ran while one was open for 65% of the time, Pallas kernels for 0%

profile of v1, /device:TPU:0, one launch (start us, length us, event | category | flops | bytes accessed | tf_op | source)
XLA Modules:
  0.0 1001.7 jit_solution(16417237607577709271)
XLA Ops:
  9.1 16.1 %add_bitcast_fusion = f32[8,16,64,128,1]{3,0,2,1,4:T(8,128)S(1)} fusion(bf16[8,31,8192]{2,0,1:T(8,128)(2,1)} %param.5, f32[8192]{0:T(1024)S(1)} %get-tuple-element.69, f32[8192]{0:T(1024)S(1)} %get-tuple-element.70, f32[8192]{0:T(1024)S(1)} %get-tuple-element.71, f32[8192]{0:T(1024)S(1)} %get-tuple-element.72, f32[8192]{0:T(1024)S(1)} %get-tuple-element.73, ...), kind=kLoop, calls=%fused_computation.26 | loop fusion | flops 49283072 | bytes 38273024 | tf_op jit(solution)/shard_map/reshape | solution.py:85
  25.2 7.2 fusion.18
  34.5 27.8 %fusion.12 = f32[8,2,2,16,64,64]{5,4,3,1,0,2:T(8,128)} fusion(f32[1,128,64]{1,2,0:T(8,128)S(1)} %get-tuple-element.92, f32[1,128,64]{1,2,0:T(8,128)S(1)} %get-tuple-element.93, f32[8,1,16,64,128]{4,3,1,2,0:T(8,128)S(1)} %get-tuple-element.51, f32[8,1,16,64,128]{4,3,1,2,0:T(8,128)S(1)} %get-tuple-element.50), kind=kOutput, calls=%fused_computation.18 | convolution fusion | flops 3223339008 | bytes 16842752 | tf_op jit(solution)/shard_map/irskm,qmj->irqsjk/dot_general | solution.py:93
  62.3 12.1 %slice_subtract_fusion = (f32[8,1,1,16,64,64]{5,4,3,1,0,2:T(8,128)}, f32[8,1,1,16,64,64]{5,4,3,1,0,2:T(8,128)}) fusion(f32[8,2,2,16,64,64]{5,4,3,1,0,2:T(8,128)} %fusion.12), kind=kLoop, calls=%fused_computation.21 | loop fusion | flops 1048576 | bytes 12582912 | tf_op jit(solution)/shard_map/sub | solution.py:94
  84.9 27.9 %copy.27 = bf16[1,4096,8,2,16]{4,3,2,1,0:T(2,128)(2,1)} copy(bf16[1,4096,8,2,16]{1,4,3,2,0:T(8,128)(2,1)S(1)} %maximum_bitcast_fusion) | data formatting | bytes 4194304 | tf_op jit(solution)/shard_map/transpose | solution.py:108
  112.8 40.3 %reshape.380 = bf16[1,16,65536]{2,1,0:T(8,128)(2,1)S(1)} reshape(bf16[1,4096,8,2,16]{4,3,2,1,0:T(2,128)(2,1)} %copy.27) | data formatting | bytes 4194304 | tf_op jit(solution)/shard_map/reshape | solution.py:109
  153.2 6.1 constant_dynamic-slice_fusion
  164.3 251.4 %multiply_convert_fusion = (bf16[8,32,1,1024,64,1]{3,4,5,2,1,0:T(8,128)(2,1)}, bf16[8,32,1,1024,64,1]{3,4,5,2,1,0:T(8,128)(2,1)}) fusion(f32[1024,64]{0,1:T(8,128)S(1)} %copy-done, f32[8,32]{1,0:T(8,128)S(1)} %add_convert_fusion), kind=kLoop, calls=%fused_computation.11 | loop fusion | flops 117440512 | bytes 67372032 | tf_op jit(solution)/shard_map/convert_element_type | solution.py:116
  425.0 229.1 %fusion.15 = bf16[8,32,1,1024,64,1]{3,4,5,2,1,0:T(8,128)(2,1)} fusion(f32[1024,64]{0,1:T(8,128)S(1)} %copy-done, f32[8,32]{1,0:T(8,128)S(1)} %add_convert_fusion), kind=kLoop, calls=%fused_computation.19 | loop fusion | flops 134217728 | bytes 33817600 | tf_op jit(solution)/shard_map/neg | solution.py:118
  663.0 86.9 %maximum_maximum_fusion = bf16[8,32,2,1024,64,2]{3,4,5,2,1,0:T(8,128)(2,1)} fusion(bf16[8,32,1,1024,64,1]{3,4,5,2,1,0:T(8,128)(2,1)} %get-tuple-element.85, bf16[8,32,1,1024,64,1]{3,4,5,2,1,0:T(8,128)(2,1)} %get-tuple-element.84, bf16[8,32,1,1024,64,1]{3,4,5,2,1,0:T(8,128)(2,1)} %fusion.15), kind=kLoop, calls=%fused_computation.10 | loop fusion | flops 201326592 | bytes 234881024 | tf_op jit(solution)/shard_map/stack | solution.py:117
  837.7 20.0 %reshape.381 = bf16[1,16,256,8,2,16]{5,4,3,2,1,0:T(2,128)(2,1)} reshape(bf16[1,16,65536]{2,1,0:T(8,128)(2,1)S(1)} %dynamic_update_slice.67) | data formatting | bytes 4194304 | tf_op jit(solution)/shard_map/reshape | solution.py:125
  857.8 35.2 %copy.28 = bf16[256,16,8,2,1,16]{0,5,3,2,1,4:T(8,128)(2,1)S(1)} copy(bf16[256,16,8,2,1,16]{5,3,2,0,1,4:T(2,128)(2,1)} %bitcast.88) | data formatting | bytes 4194304 | tf_op jit(solution)/shard_map/transpose | solution.py:126
  893.0 6.3 reshape.382
  899.2 13.3 %copy.29 = bf16[8,32,64,2,2,1,16]{2,6,4,3,1,5,0:T(8,128)(2,1)} copy(bf16[8,32,64,2,2,1,16]{1,0,6,4,3,2,5:T(8,128)(2,1)} %reshape.382) | data formatting | bytes 4194304 | tf_op jit(solution)/shard_map/while | solution.py:137
  912.6 59.1 %while.10 = (s32[]{:T(128)}, bf16[8,32,1024,1]{2,3,1,0:T(2,128)(2,1)S(1)}, bf16[8,32,2,1024,64,2]{3,4,5,2,1,0:T(8,128)(2,1)}, bf16[8,32,64,2,2,1,16]{2,6,4,3,1,5,0:T(8,128)(2,1)}, s32[]{:T(128)}) while((s32[]{:T(128)}, bf16[8,32,1024,1]{2,3,1,0:T(2,128)(2,1)S(1)}, bf16[8,32,2,1024,64,2]{3,4,5,2,1,0:T(8,128)(2,1)}, ...), condition=%wide.region_3.4_spmd, body=%wide.region_1.3_spmd.sunk | while | flops 541097984 | bytes 17826888 | solution.py:137
  912.6 7.2 fusion.68
  920.0 7.3 fusion.68
  927.4 7.3 fusion.68
  934.7 7.3 fusion.68
  942.1 7.2 fusion.68
  949.5 7.2 fusion.68
  956.9 7.3 fusion.68
  964.3 7.3 fusion.68
  977.3 19.4 %all_to_all.5 = bf16[16,2,8192]{2,1,0:T(2,128)(2,1)S(1)} all-to-all(bf16[16,2,8192]{2,1,0:T(2,128)(2,1)S(1)} %reshape.395), channel_id=1, replica_groups=mesh['grp'=2,'chan'=16] {'chan'}, dimensions={0} | all-to-all | bytes 1048576 | tf_op jit(solution)/shard_map/all_to_all | solution.py:140
  (129 shorter events, 142.3 us)
Async XLA Ops:
  159.3 256.4 %collective-permute-start = (bf16[1,1,65536]{2,1,0:T(2,128)(2,1)}, bf16[1,1,65536]{2,1,0:T(2,128)(2,1)S(1)}, u32[]{:S(2)}, u32[]{:S(2)}) collective-permute-start(bf16[1,1,65536]{2,1,0:T(2,128)(2,1)} %get-tuple-element.66), channel_id=1, source_target_pairs={{0,1},{1,0},{2,3},{3,2},{4,5},{5,4},{6,7},{7,6},{8,9},{9,8},{10,11... | collective-permute-start | bytes 393224 | tf_op jit(solution)/shard_map/ppermute | solution.py:27
  159.8 258.5 %collective-permute-start.1 = (bf16[1,1,65536]{2,1,0:T(2,128)(2,1)}, bf16[1,1,65536]{2,1,0:T(2,128)(2,1)S(1)}, u32[]{:S(2)}, u32[]{:S(2)}) collective-permute-start(bf16[1,1,65536]{2,1,0:T(2,128)(2,1)} %get-tuple-element.65), channel_id=1, source_target_pairs={{0,2},{1,3},{2,0},{3,1},{4,6},{5,7},{6,4},{7,5},{8,10},{9,11},{10,... | collective-permute-start | bytes 393224 | tf_op jit(solution)/shard_map/ppermute | solution.py:27
  162.4 256.2 %collective-permute-start.2 = (bf16[1,1,65536]{2,1,0:T(2,128)(2,1)}, bf16[1,1,65536]{2,1,0:T(2,128)(2,1)S(1)}, u32[]{:S(2)}, u32[]{:S(2)}) collective-permute-start(bf16[1,1,65536]{2,1,0:T(2,128)(2,1)} %get-tuple-element.64), channel_id=1, source_target_pairs={{0,3},{1,2},{2,1},{3,0},{4,7},{5,6},{6,5},{7,4},{8,11},{9,10},{10,... | collective-permute-start | bytes 393224 | tf_op jit(solution)/shard_map/ppermute | solution.py:27
  162.4 258.9 %collective-permute-start.3 = (bf16[1,1,65536]{2,1,0:T(2,128)(2,1)}, bf16[1,1,65536]{2,1,0:T(2,128)(2,1)S(1)}, u32[]{:S(2)}, u32[]{:S(2)}) collective-permute-start(bf16[1,1,65536]{2,1,0:T(2,128)(2,1)} %get-tuple-element.63), channel_id=1, source_target_pairs={{0,4},{1,5},{2,6},{3,7},{4,0},{5,1},{6,2},{7,3},{8,12},{9,13},{10,... | collective-permute-start | bytes 393224 | tf_op jit(solution)/shard_map/ppermute | solution.py:27
  164.2 257.2 %collective-permute-start.4 = (bf16[1,1,65536]{2,1,0:T(2,128)(2,1)}, bf16[1,1,65536]{2,1,0:T(2,128)(2,1)S(1)}, u32[]{:S(2)}, u32[]{:S(2)}) collective-permute-start(bf16[1,1,65536]{2,1,0:T(2,128)(2,1)} %get-tuple-element.62), channel_id=1, source_target_pairs={{0,5},{1,4},{2,7},{3,6},{4,1},{5,0},{6,3},{7,2},{8,13},{9,12},{10,... | collective-permute-start | bytes 393224 | tf_op jit(solution)/shard_map/ppermute | solution.py:27
  164.2 251.5 %copy-start.6 = (bf16[1,1,65536]{2,1,0:T(2,128)(2,1)S(1)}, bf16[1,1,65536]{2,1,0:T(2,128)(2,1)}, u32[]{:S(2)}) copy-start(bf16[1,1,65536]{2,1,0:T(2,128)(2,1)} %get-tuple-element.61) | copy-start | bytes 393220
  164.2 254.2 %copy-start.5 = (bf16[1,1,65536]{2,1,0:T(2,128)(2,1)S(1)}, bf16[1,1,65536]{2,1,0:T(2,128)(2,1)}, u32[]{:S(2)}) copy-start(bf16[1,1,65536]{2,1,0:T(2,128)(2,1)} %get-tuple-element.60) | copy-start | bytes 393220
  164.2 254.3 %copy-start.4 = (bf16[1,1,65536]{2,1,0:T(2,128)(2,1)S(1)}, bf16[1,1,65536]{2,1,0:T(2,128)(2,1)}, u32[]{:S(2)}) copy-start(bf16[1,1,65536]{2,1,0:T(2,128)(2,1)} %get-tuple-element.59) | copy-start | bytes 393220
  164.2 257.1 %copy-start.3 = (bf16[1,1,65536]{2,1,0:T(2,128)(2,1)S(1)}, bf16[1,1,65536]{2,1,0:T(2,128)(2,1)}, u32[]{:S(2)}) copy-start(bf16[1,1,65536]{2,1,0:T(2,128)(2,1)} %get-tuple-element.58) | copy-start | bytes 393220
  164.2 257.1 %copy-start.2 = (bf16[1,1,65536]{2,1,0:T(2,128)(2,1)S(1)}, bf16[1,1,65536]{2,1,0:T(2,128)(2,1)}, u32[]{:S(2)}) copy-start(bf16[1,1,65536]{2,1,0:T(2,128)(2,1)} %get-tuple-element.57) | copy-start | bytes 393220
  415.7 238.4 %copy-start.7 = (bf16[1,1,65536]{2,1,0:T(2,128)(2,1)}, bf16[1,1,65536]{2,1,0:T(2,128)(2,1)S(1)}, u32[]{:S(2)}) copy-start(bf16[1,1,65536]{2,1,0:T(2,128)(2,1)S(1)} %collective-permute-done) | copy-start | bytes 393220
  415.7 238.4 %collective-permute-start.5 = (bf16[1,1,65536]{2,1,0:T(2,128)(2,1)S(1)}, bf16[1,1,65536]{2,1,0:T(2,128)(2,1)S(1)}, u32[]{:S(2)}, u32[]{:S(2)}) collective-permute-start(bf16[1,1,65536]{2,1,0:T(2,128)(2,1)S(1)} %copy-done.6), channel_id=1, source_target_pairs={{0,6},{1,7},{2,4},{3,5},{4,2},{5,3},{6,0},{7,1},{8,14},{9,15},{10,... | collective-permute-start | bytes 393224 | tf_op jit(solution)/shard_map/ppermute | solution.py:27
  418.4 235.7 %copy-start.9 = (bf16[1,1,65536]{2,1,0:T(2,128)(2,1)}, bf16[1,1,65536]{2,1,0:T(2,128)(2,1)S(1)}, u32[]{:S(2)}) copy-start(bf16[1,1,65536]{2,1,0:T(2,128)(2,1)S(1)} %collective-permute-done.1) | copy-start | bytes 393220
  418.4 235.9 %collective-permute-start.6 = (bf16[1,1,65536]{2,1,0:T(2,128)(2,1)S(1)}, bf16[1,1,65536]{2,1,0:T(2,128)(2,1)S(1)}, u32[]{:S(2)}, u32[]{:S(2)}) collective-permute-start(bf16[1,1,65536]{2,1,0:T(2,128)(2,1)S(1)} %copy-done.5), channel_id=1, source_target_pairs={{0,7},{1,6},{2,5},{3,4},{4,3},{5,2},{6,1},{7,0},{8,15},{9,14},{10,... | collective-permute-start | bytes 393224 | tf_op jit(solution)/shard_map/ppermute | solution.py:27
  418.5 235.5 %copy-start.10 = (bf16[1,1,65536]{2,1,0:T(2,128)(2,1)}, bf16[1,1,65536]{2,1,0:T(2,128)(2,1)S(1)}, u32[]{:S(2)}) copy-start(bf16[1,1,65536]{2,1,0:T(2,128)(2,1)S(1)} %collective-permute-done.2) | copy-start | bytes 393220
  418.5 239.4 %collective-permute-start.7 = (bf16[1,1,65536]{2,1,0:T(2,128)(2,1)S(1)}, bf16[1,1,65536]{2,1,0:T(2,128)(2,1)S(1)}, u32[]{:S(2)}, u32[]{:S(2)}) collective-permute-start(bf16[1,1,65536]{2,1,0:T(2,128)(2,1)S(1)} %copy-done.4), channel_id=1, source_target_pairs={{0,8},{1,9},{2,10},{3,11},{4,12},{5,13},{6,14},{7,15},{8,0},{9,1},... | collective-permute-start | bytes 393224 | tf_op jit(solution)/shard_map/ppermute | solution.py:27
  421.3 232.8 %copy-start.11 = (bf16[1,1,65536]{2,1,0:T(2,128)(2,1)}, bf16[1,1,65536]{2,1,0:T(2,128)(2,1)S(1)}, u32[]{:S(2)}) copy-start(bf16[1,1,65536]{2,1,0:T(2,128)(2,1)S(1)} %collective-permute-done.3) | copy-start | bytes 393220
  421.3 236.7 %collective-permute-start.8 = (bf16[1,1,65536]{2,1,0:T(2,128)(2,1)S(1)}, bf16[1,1,65536]{2,1,0:T(2,128)(2,1)S(1)}, u32[]{:S(2)}, u32[]{:S(2)}) collective-permute-start(bf16[1,1,65536]{2,1,0:T(2,128)(2,1)S(1)} %copy-done.3), channel_id=1, source_target_pairs={{0,9},{1,8},{2,11},{3,10},{4,13},{5,12},{6,15},{7,14},{8,1},{9,0},... | collective-permute-start | bytes 393224 | tf_op jit(solution)/shard_map/ppermute | solution.py:27
  421.4 240.9 %collective-permute-start.9 = (bf16[1,1,65536]{2,1,0:T(2,128)(2,1)S(1)}, bf16[1,1,65536]{2,1,0:T(2,128)(2,1)S(1)}, u32[]{:S(2)}, u32[]{:S(2)}) collective-permute-start(bf16[1,1,65536]{2,1,0:T(2,128)(2,1)S(1)} %copy-done.2), channel_id=1, source_target_pairs={{0,10},{1,11},{2,8},{3,9},{4,14},{5,15},{6,12},{7,13},{8,2},{9,3},... | collective-permute-start | bytes 393224 | tf_op jit(solution)/shard_map/ppermute | solution.py:27
  654.1 154.4 %collective-permute-start.10 = (bf16[1,1,65536]{2,1,0:T(2,128)(2,1)}, bf16[1,1,65536]{2,1,0:T(2,128)(2,1)}, u32[]{:S(2)}, u32[]{:S(2)}) collective-permute-start(bf16[1,1,65536]{2,1,0:T(2,128)(2,1)} %get-tuple-element.56), channel_id=1, source_target_pairs={{0,11},{1,10},{2,9},{3,8},{4,15},{5,14},{6,13},{7,12},{8,3},{9,2},... | collective-permute-start | bytes 393224 | tf_op jit(solution)/shard_map/ppermute | solution.py:27
  654.3 160.2 %collective-permute-start.11 = (bf16[1,1,65536]{2,1,0:T(2,128)(2,1)}, bf16[1,1,65536]{2,1,0:T(2,128)(2,1)}, u32[]{:S(2)}, u32[]{:S(2)}) collective-permute-start(bf16[1,1,65536]{2,1,0:T(2,128)(2,1)} %get-tuple-element.55), channel_id=1, source_target_pairs={{0,12},{1,13},{2,14},{3,15},{4,8},{5,9},{6,10},{7,11},{8,4},{9,5},... | collective-permute-start | bytes 393224 | tf_op jit(solution)/shard_map/ppermute | solution.py:27
  657.9 162.4 %collective-permute-start.12 = (bf16[1,1,65536]{2,1,0:T(2,128)(2,1)S(1)}, bf16[1,1,65536]{2,1,0:T(2,128)(2,1)}, u32[]{:S(2)}, u32[]{:S(2)}) collective-permute-start(bf16[1,1,65536]{2,1,0:T(2,128)(2,1)S(1)} %get-tuple-element.54), channel_id=1, source_target_pairs={{0,13},{1,12},{2,15},{3,14},{4,9},{5,8},{6,11},{7,10},{8,5},{9,4},... | collective-permute-start | bytes 393224 | tf_op jit(solution)/shard_map/ppermute | solution.py:27
  658.0 168.1 %collective-permute-start.13 = (bf16[1,1,65536]{2,1,0:T(2,128)(2,1)S(1)}, bf16[1,1,65536]{2,1,0:T(2,128)(2,1)}, u32[]{:S(2)}, u32[]{:S(2)}) collective-permute-start(bf16[1,1,65536]{2,1,0:T(2,128)(2,1)S(1)} %get-tuple-element.53), channel_id=1, source_target_pairs={{0,14},{1,15},{2,12},{3,13},{4,10},{5,11},{6,8},{7,9},{8,6},{9,7},... | collective-permute-start | bytes 393224 | tf_op jit(solution)/shard_map/ppermute | solution.py:27
  662.3 169.6 %collective-permute-start.14 = (bf16[1,1,65536]{2,1,0:T(2,128)(2,1)S(1)}, bf16[1,1,65536]{2,1,0:T(2,128)(2,1)}, u32[]{:S(2)}, u32[]{:S(2)}) collective-permute-start(bf16[1,1,65536]{2,1,0:T(2,128)(2,1)S(1)} %get-tuple-element.52), channel_id=1, source_target_pairs={{0,15},{1,14},{2,13},{3,12},{4,11},{5,10},{6,9},{7,8},{8,7},{9,6},... | collective-permute-start | bytes 393224 | tf_op jit(solution)/shard_map/ppermute | solution.py:27
  (12 other events, 732.1 us)
